TPU v7x, 128 devices: a whole 4x4x4 slice. The times are simulated.
128 devices in a mesh: replica: 8 (over z_lo, y), space: 16 (over z_hi, x, core).
Axes of the slice: x: 4, y: 4, z: 4 (z_hi: 2, z_lo: 2; z = z_hi * 2 + z_lo), core: 2. Of those that a mesh axis runs over, the one named last changes fastest.
Arguments:
- inputs: bfloat16 [8, 128, 512, 256], P('replica', 'space'), may hold values from -6 to 6
- cotangent: bfloat16 [8, 128, 512, 256], P('replica', 'space'), may hold values from -6 to 6
- land_mask: int32 [128, 512], P('space'), may hold values 0 or 1
- weights: float32 [8, 2, 2304, 256], P('replica', None, 'space'), may hold values from -0.125 to 0.125
- momentum: float32 [8, 2, 2304, 256], P('replica', None, 'space'), may hold values from -6 to 6
- step: int32 [1], replicated, may hold values from 0 to 63
Outputs:
- grad_input: bfloat16 [8, 128, 512, 256], P('replica', 'space')
- new_weights: float32 [8, 2, 2304, 256], P('replica', None, 'space')
- new_momentum: float32 [8, 2, 2304, 256], P('replica', None, 'space')
All inputs are finite; a program needn't handle non-finite values. No bound on the sum of `land_mask` on one device may be relied on, other than what follows from the above.
Results may differ from a plain program's by a relative error of at most 0.012.
Values may be sent and summed in bfloat16 or wider, within the bound.
No kernel may reach another device: no remote copies, remote signals or barrier semaphores. Data moves between devices by JAX's collectives and lax.ppermute only.
A program may use at most 256 MiB of HBM per device.

v0:
```python
from functools import partial
import math

import jax
import jax.numpy as jnp
from jax import lax
from jax.sharding import PartitionSpec as P


def extended_2(shard, sides, width):
    for axis, dim in sides:
        size, length = (lax.axis_size(axis), shard.shape[dim])
        up = [(i, (i + 1) % size) for i in range(size - 1)]
        down = [(j, i) for i, j in up]
        last = lax.slice_in_dim(shard, length - width, length, axis=dim)
        initial = lax.slice_in_dim(shard, 0, width, axis=dim)
        before = lax.ppermute(last, axis, up)
        after = lax.ppermute(initial, axis, down)
        shard = jnp.concatenate([before, shard, after], axis=dim)
    return shard


def as_sent(shard):

    def short(part):
        return part.astype(jnp.bfloat16) if part.dtype == jnp.float32 else part

    return jax.tree.map(short, shard)


def passed_along(shard, axis, by):
    length = lax.axis_size(axis)
    return lax.ppermute(shard, axis, [(i, (i + by) % length) for i in range(length)])


def conv_ahead(extended, kernel):
    chan_count = extended.shape[-1]
    taps = kernel.reshape(3, 3, chan_count, kernel.shape[1])
    return lax.conv_general_dilated(
        extended[None],
        taps,
        (1, 1),
        ((0, 0), (1, 1)),
        dimension_numbers=("NHWC", "HWIO", "NHWC"),
        preferred_element_type=jnp.float32,
    )[0]


def conv_behind(extended, kernel):
    chan_count = kernel.shape[0] // 9
    taps = jnp.flip(kernel.reshape(3, 3, chan_count, kernel.shape[1]), (0, 1))
    return lax.conv_general_dilated(
        extended[None],
        taps,
        (1, 1),
        ((0, 0), (1, 1)),
        dimension_numbers=("NHWC", "HWOI", "NHWC"),
        preferred_element_type=jnp.float32,
    )[0]


def kernel_grad(extended, upstream):
    grad = lax.conv_general_dilated(
        extended[None],
        upstream[None],
        (1, 1),
        ((0, 0), (1, 1)),
        dimension_numbers=("CHWN", "IHWO", "HWNC"),
        preferred_element_type=jnp.float32,
    )
    return grad.reshape(-1, grad.shape[-1])


def kernel_grad_behind(extended_upstream, field):
    grad = lax.conv_general_dilated(
        extended_upstream[None],
        field[None],
        (1, 1),
        ((0, 0), (1, 1)),
        dimension_numbers=("CHWN", "IHWO", "HWCN"),
        preferred_element_type=jnp.float32,
    )
    grad = jnp.flip(grad, (0, 1))
    return grad.reshape(-1, grad.shape[-1])


def silu_slope(preact):
    sigma = jax.nn.sigmoid(preact)
    return sigma * (1.0 + preact * (1.0 - sigma))


def rim(stacked):
    return extended_2(stacked, (("space", 1),), 1)


def send_both(distance, stacked):
    return jax.tree.map(
        lambda part, own: part.astype(own.dtype),
        passed_along(as_sent(stacked), "replica", distance),
        stacked,
    )


def gossip(step, stacked, sender):
    levels = lax.axis_size("replica").bit_length() - 1
    received = lax.switch(
        step[0] % levels, [partial(sender, 1 << power) for power in range(levels)], stacked
    )
    return 0.5 * (stacked + received)


def swapped(part, bit):
    count = lax.axis_size("space")
    return lax.ppermute(part, "space", [(i, i ^ (1 << bit)) for i in range(count)])


def space_bits():
    return lax.axis_size("space").bit_length() - 1


def gathered_kernels(weights):
    count = lax.axis_size("space")
    own = weights[0].astype(jnp.bfloat16)
    copies = jnp.broadcast_to(own[None], (count,) + own.shape)
    have = lax.all_to_all(copies, "space", 0, 0, tiled=True)
    kernels = jnp.moveaxis(have, 0, 1)
    return kernels.reshape(kernels.shape[0], -1, kernels.shape[-1])


def scattered(grad):
    count = lax.axis_size("space")
    blocks = grad.reshape((grad.shape[0], count, -1) + grad.shape[2:])
    received = lax.all_to_all(
        jnp.moveaxis(blocks, 1, 0).astype(jnp.bfloat16), "space", 0, 0, tiled=True
    )
    return jnp.sum(received.astype(jnp.float32), axis=0)


def shards(inputs, cotangent, land_mask, weights, momentum, step):
    row_count = inputs.shape[1]
    col_count = inputs.shape[2]
    space_count = lax.axis_size("space")
    scale = 1.0 / math.sqrt(row_count * space_count * col_count)
    masked = cotangent[0] * land_mask.astype(jnp.bfloat16)[:, :, None]
    kernels = gathered_kernels(weights)
    kernel_first = kernels[0]
    kernel_second = kernels[1]
    paired = rim(jnp.stack([inputs[0], masked]))
    input_ext = paired[0]
    masked_ext = paired[1]
    preact = conv_ahead(input_ext, kernel_first)
    hidden = jax.nn.silu(preact).astype(jnp.bfloat16)
    share_second = scattered(kernel_grad_behind(masked_ext, hidden)[None] * scale)
    back_mid = (conv_behind(masked_ext, kernel_second) * silu_slope(preact)).astype(jnp.bfloat16)
    grad_first = kernel_grad(input_ext, back_mid) * scale
    back_ext, grad_first = lax.optimization_barrier((rim(back_mid[None])[0], grad_first))
    grad_input = (conv_behind(back_ext, kernel_first) + masked.astype(jnp.float32)).astype(
        jnp.bfloat16
    )[None]
    shares = jnp.stack([scattered(grad_first[None])[0], share_second[0]])[None]
    moment = 0.9 * momentum + shares
    updated = weights - 0.01 * moment
    mixed = gossip(step, jnp.stack([updated, moment]), send_both)
    new_weights = mixed[0]
    new_momentum = mixed[1]
    return (grad_input, new_weights, new_momentum)


def solution(mesh):
    in_specs = (
        P("replica", "space", None, None),
        P("replica", "space", None, None),
        P("space", None),
        P("replica", None, "space", None),
        P("replica", None, "space", None),
        P(),
    )
    out_specs = (
        P("replica", "space", None, None),
        P("replica", None, "space", None),
        P("replica", None, "space", None),
    )
    return jax.shard_map(shards, mesh=mesh, in_specs=in_specs, out_specs=out_specs, check_vma=False)
```

profile of v0, /device:TPU:0, one launch (start us, length us, event | category | flops | bytes accessed | tf_op | source)
XLA Modules:
  0.0 202.5 jit_solution(6143669131269259040)
XLA Ops:
  1.5 2.9 %copy.51 = bf16[1,8,512,256]{3,1,2,0:T(8,128)(2,1)S(1)} copy(bf16[1,8,512,256]{3,2,1,0:T(8,128)(2,1)} %param.9) | data formatting | bytes 4194304 | tf_op args[0]
  4.5 3.1 %copy_multiply_fusion = bf16[1,8,512,256]{3,1,2,0:T(8,128)(2,1)S(1)} fusion(bf16[1,8,512,256]{3,2,1,0:T(8,128)(2,1)S(1)} %copy-done.8, bf16[8,512]{0,1:T(8,128)(2,1)S(1)} %copy.49), kind=kLoop, calls=%fused_computation.70 | loop fusion | flops 1048576 | bytes 4202496 | tf_op jit(solution)/shard_map/mul | solution.py:144
  14.4 12.3 %all-to-all-start = ((bf16[16,2,144,256]{3,2,1,0:T(8,128)(2,1)}), bf16[16,2,144,256]{3,2,1,0:T(8,128)(2,1)}, u32[]{:S(2)}, u32[]{:S(2)}) async-start(bf16[16,2,144,256]{3,2,1,0:T(8,128)(2,1)} %broadcast_in_dim.9), calls=%async_computation | async-start | bytes 4718592 | tf_op jit(solution)/shard_map/all_to_all | solution.py:125
  30.0 6.1 %pad_maximum_fusion = bf16[2,10,512,256]{3,1,2,0:T(8,128)(2,1)S(1)} fusion(bf16[2,1,512,256]{3,1,2,0:T(2,128)(2,1)S(1)} %copy.55, bf16[1,8,512,256]{3,1,2,0:T(8,128)(2,1)S(1)} %copy-done.5, bf16[1,8,512,256]{3,1,2,0:T(8,128)(2,1)S(1)} %copy.51, bf16[2,1,512,256]{3,1,2,0:T(2,128)(2,1)S(1)} %copy.54), kind=kLoop, calls=%fused_computation | loop fusion | flops 20971520 | bytes 10485760 | tf_op jit(solution)/shard_map/concatenate | solution.py:19
  36.2 2.3 %slice_bitcast_fusion.2 = (bf16[10,1,512,256]{3,0,2,1:T(8,128)(2,1)S(1)}, bf16[10,1,512,256]{3,0,2,1:T(8,128)(2,1)}) fusion(bf16[2,10,512,256]{3,1,2,0:T(8,128)(2,1)S(1)} %pad_maximum_fusion), kind=kLoop, calls=%fused_computation.30 | loop fusion | bytes 10485760 | tf_op jit(solution)/shard_map/slice | solution.py:150
  40.7 3.0 %reshape.67 = bf16[10,1,8,65,256]{4,3,2,0,1:T(8,128)(2,1)} reshape(bf16[10,1,520,256]{3,2,0,1:T(8,128)(2,1)S(1)} %pad.4.clone) | data formatting | bytes 5324800 | tf_op jit(solution)/shard_map/slice | solution.py:150
  43.7 3.0 %reshape.72 = bf16[10,8,65,256,1]{3,2,1,0,4:T(8,128)(2,1)} reshape(bf16[10,1,520,256]{3,2,0,1:T(8,128)(2,1)S(1)} %pad.4.clone) | data formatting | bytes 5324800 | tf_op jit(solution)/shard_map/slice | solution.py:150
  46.7 4.9 %pad.2 = bf16[10,1,520,256]{3,0,2,1:T(8,128)(2,1)} pad(bf16[10,1,512,256]{3,0,2,1:T(8,128)(2,1)} %get-tuple-element.27, bf16[]{:T(256)} %constant.35), padding=0_0x0_0x1_7x0_0 | pad | bytes 5283842 | tf_op jit(solution)/shard_map/slice | solution.py:149
  53.8 2.6 %pad = bf16[10,1,520,256]{3,0,2,1:T(8,128)(2,1)} pad(bf16[10,1,512,256]{3,0,2,1:T(8,128)(2,1)S(1)} %copy-done.1, bf16[]{:T(256)} %constant.35), padding=0_0x0_0x1_7x0_0 | pad | bytes 5283842 | tf_op jit(solution)/shard_map/slice | solution.py:150
  56.5 3.0 %reshape.83 = bf16[10,1,8,65,256]{4,3,2,0,1:T(8,128)(2,1)} reshape(bf16[10,1,520,256]{3,2,0,1:T(8,128)(2,1)S(1)} %pad.7.clone) | data formatting | bytes 5324800 | tf_op jit(solution)/shard_map/slice | solution.py:149
  59.5 3.5 %reshape.88 = bf16[10,8,65,256,1]{3,2,1,0,4:T(8,128)(2,1)} reshape(bf16[10,1,520,256]{3,2,0,1:T(8,128)(2,1)S(1)} %pad.7.clone) | data formatting | bytes 5324800 | tf_op jit(solution)/shard_map/slice | solution.py:149
  63.0 4.2 %fusion.93 = (bf16[10,1,8,64,256]{4,3,2,0,1:T(8,128)(2,1)S(1)}, bf16[10,1,8,64,256]{4,3,2,0,1:T(8,128)(2,1)S(1)}) fusion(bf16[10,1,8,65,256]{4,3,2,0,1:T(8,128)(2,1)} %reshape.67), kind=kLoop, calls=%fused_computation.104 | loop fusion | bytes 10485760 | tf_op jit(solution)/shard_map/slice | solution.py:150
  73.7 2.0 %copy.85 = bf16[10,8,65,256,1]{3,1,4,2,0:T(8,128)(2,1)} copy(bf16[10,8,65,256,1]{3,2,1,0,4:T(8,128)(2,1)S(1)} %copy-done.7) | data formatting | bytes 5324800 | tf_op jit(solution)/shard_map/slice | solution.py:150
  76.2 1.9 fusion.95
  83.7 2.1 %copy.73 = bf16[10,8,65,256,1]{3,1,4,2,0:T(8,128)(2,1)} copy(bf16[10,8,65,256,1]{3,2,1,0,4:T(8,128)(2,1)S(1)} %copy-done.6) | data formatting | bytes 5324800 | tf_op jit(solution)/shard_map/slice | solution.py:149
  85.8 2.5 %fusion.45 = (bf16[10,8,65,256,1]{3,1,4,2,0:T(8,128)(2,1)}, bf16[10,8,65,256,1]{3,1,4,2,0:T(8,128)(2,1)}) fusion(bf16[10,1,7,1,256]{4,2,3,0,1:T(8,128)(2,1)S(1)} %copy.100, bf16[10,1,8,64,256]{4,2,3,0,1:T(8,128)(2,1)S(1)} %copy.101, bf16[10,1,7,1,256]{4,2,3,0,1:T(8,128)(2,1)S(1)} %copy.103, bf16[10,1,8,64,256]{4,2,3,0,1:T(8,128)(2,1)S(1)} %copy.102), kind=kLoop, calls=%fused_computation.53 | loop fusion | flops 15974400 | bytes 10639360 | tf_op jit(solution)/shard_map/slice | solution.py:150
  88.3 2.5 %fusion.43 = (bf16[10,8,65,256,1]{3,1,4,2,0:T(8,128)(2,1)}, bf16[10,8,65,256,1]{3,1,4,2,0:T(8,128)(2,1)}) fusion(bf16[10,1,7,1,256]{4,2,3,0,1:T(8,128)(2,1)S(1)} %copy.96, bf16[10,1,8,64,256]{4,2,3,0,1:T(8,128)(2,1)S(1)} %copy.97, bf16[10,1,7,1,256]{4,2,3,0,1:T(8,128)(2,1)S(1)} %copy.99, bf16[10,1,8,64,256]{4,2,3,0,1:T(8,128)(2,1)S(1)} %copy.98), kind=kLoop, calls=%fused_computation.51 | loop fusion | flops 15974400 | bytes 10639360 | tf_op jit(solution)/shard_map/slice | solution.py:149
  90.9 2.8 %fusion.97 = (bf16[1,16,144,256]{3,2,0,1:T(8,128)(2,1)}, bf16[1,16,144,256]{3,2,0,1:T(8,128)(2,1)S(1)}) fusion(bf16[2,16,144,256]{3,2,0,1:T(8,128)(2,1)} %bitcast.4), kind=kLoop, calls=%fused_computation.108 | loop fusion | bytes 4718592 | tf_op jit(solution)/shard_map/slice | solution.py:147
  93.7 5.4 %fusion.27 = f32[8,8,65,256]{3,1,2,0:T(8,128)S(1)} fusion(bf16[3,3,256,256]{3,2,1,0:T(8,128)(2,1)S(1)} %bitcast.115, bf16[10,1,7,2,256]{4,2,3,0,1:T(8,128)(2,1)S(1)} %slice.63, bf16[10,1,8,65,256]{4,2,3,0,1:T(8,128)(2,1)S(1)} %copy.61), kind=kOutput, calls=%fused_computation.37 | convolution fusion | flops 4915568640 | bytes 8173568 | tf_op jit(solution)/shard_map/conv_general_dilated | solution.py:39
  99.1 8.6 %fusion.66 = f32[3,3,256,256]{2,3,1,0:T(8,128)S(1)} fusion(f32[8,8,65,256]{3,1,2,0:T(8,128)S(1)} %fusion.27, pred[8,65]{0,1:T(8,128)(4,1)S(1)} %copy-done.23, bf16[10,8,65,256,1]{3,1,4,2,0:T(8,128)(2,1)S(1)} %copy-done.14, bf16[10,8,65,256,1]{3,1,4,2,0:T(8,128)(2,1)S(1)} %copy-done.12, bf16[10,8,65,256,1]{3,1,4,2,0:T(8,128)(2,1)S(1)} %copy-done.13), kind=kOutput, calls=%fused_computation.72 | convolution fusion | flops 4922777600 | bytes 14606856 | tf_op jit(solution)/shard_map/conv_general_dilated | solution.py:75
  109.5 7.3 %all-to-all-start.2 = ((bf16[16,1,144,256]{3,2,1,0:T(8,128)(2,1)}), bf16[16,1,144,256]{3,2,1,0:T(8,128)(2,1)S(1)}, u32[]{:S(2)}, u32[]{:S(2)}) async-start(bf16[16,1,144,256]{3,2,1,0:T(8,128)(2,1)} %bitcast.31), calls=%async_computation.2 | async-start | bytes 2359296 | tf_op jit(solution)/shard_map/all_to_all | solution.py:133
  116.8 9.6 %multiply_convert_fusion = bf16[8,8,65,256]{3,1,2,0:T(8,128)(2,1)S(1)} fusion(f32[8,8,65,256]{3,1,2,0:T(8,128)} %copy-done.24, bf16[3,3,256,256]{3,2,1,0:T(8,128)(2,1)} %bitcast.117, bf16[10,1,7,2,256]{4,2,3,0,1:T(8,128)(2,1)S(1)} %copy-done.22, bf16[10,1,8,65,256]{4,2,3,0,1:T(8,128)(2,1)} %copy-done.10, pred[8,65]{0,1:T(8,128)(4,1)S(1)} %copy-done.23), kind=kOutput, calls=%fused_computation.23 | convolution fusion | flops 4927283200 | bytes 10304008 | tf_op jit(solution)/shard_map/conv_general_dilated | solution.py:52
  129.8 2.4 %slice.69 = bf16[1,1,512,256]{3,1,2,0:T(2,128)(2,1)} slice(bf16[1,1,520,256]{3,1,2,0:T(2,128)(2,1)} %reshape.136), slice={[0:1], [0:1], [0:512], [0:256]} | slice | bytes 524288 | tf_op jit(solution)/shard_map/convert_element_type | solution.py:154
  137.9 3.0 %collective-permute-start.5 = (bf16[1,1,512,256]{3,2,1,0:T(8,128)(2,1)S(1)}, bf16[1,1,512,256]{3,2,1,0:T(8,128)(2,1)S(1)}, u32[]{:S(2)}, u32[]{:S(2)}) collective-permute-start(bf16[1,1,512,256]{3,2,1,0:T(8,128)(2,1)S(1)} %slice.66), channel_id=1, source_target_pairs={{0,1},{1,2},{2,3},{3,4},{4,5},{5,6},{6,7},{7,8},{8,9},{9,10},{10,1... | collective-permute-start | bytes 786440 | tf_op jit(solution)/shard_map/ppermute | solution.py:17
  140.9 11.8 %fusion.61 = bf16[3,3,256,256,1]{3,2,1,4,0:T(8,128)(2,1)} fusion(bf16[8,8,65,256]{3,1,2,0:T(8,128)(2,1)S(1)} %multiply_convert_fusion, pred[8,65]{0,1:T(8,128)(4,1)S(1)} %copy-done.23, bf16[10,8,65,256,1]{3,1,4,2,0:T(8,128)(2,1)} %get-tuple-element.47, bf16[10,8,65,256,1]{3,1,4,2,0:T(8,128)(2,1)} %copy.73, bf16[10,8,65,256,1]{3,1,4,2,0:T(8,128)(2,1)} %get-tuple-element.46), kind=kOutput, calls=%fused_computation.71 | convolution fusion | flops 4917567488 | bytes 11297288 | tf_op jit(solution)/shard_map/conv_general_dilated | solution.py:63
  153.8 3.9 %maximum_bitcast_fusion = bf16[10,512,256]{2,0,1:T(8,128)(2,1)S(1)} fusion(bf16[1,1,512,256]{3,1,2,0:T(2,128)(2,1)} %collective-permute-done.6, bf16[1,8,512,256]{3,1,2,0:T(8,128)(2,1)S(1)} %slice_bitcast_fusion.3, bf16[1,1,512,256]{3,1,2,0:T(2,128)(2,1)S(1)} %copy.66), kind=kLoop, calls=%fused_computation.31 | loop fusion | flops 7864320 | bytes 5242880 | tf_op jit(solution)/shard_map/squeeze | solution.py:156
  161.4 9.3 %all-to-all-start.1 = ((bf16[16,1,144,256]{3,2,1,0:T(8,128)(2,1)}), bf16[16,1,144,256]{3,2,1,0:T(8,128)(2,1)S(1)}, u32[]{:S(2)}, u32[]{:S(2)}) async-start(bf16[16,1,144,256]{3,2,1,0:T(8,128)(2,1)} %bitcast.23), calls=%async_computation.1 | async-start | bytes 2359296 | tf_op jit(solution)/shard_map/all_to_all | solution.py:133
  170.7 7.3 %broadcast_select_fusion = f32[8,8,65,256]{3,1,2,0:T(8,128)S(1)} fusion(pred[8,65]{0,1:T(8,128)(4,1)S(1)} %copy-done.23, bf16[3,3,256,256]{3,2,1,0:T(8,128)(2,1)S(1)} %bitcast.116, bf16[10,1,7,2,256]{4,2,3,0,1:T(8,128)(2,1)} %slice.74, bf16[10,1,8,65,256]{4,2,3,0,1:T(8,128)(2,1)} %copy-done.11), kind=kOutput, calls=%fused_computation.65 | convolution fusion | flops 4916633600 | bytes 8174088 | tf_op jit(solution)/shard_map/conv_general_dilated | solution.py:52
  179.6 3.1 %fusion.20 = bf16[1,8,512,256]{3,1,2,0:T(8,128)(2,1)S(1)} fusion(f32[8,1,520,256]{3,0,2,1:T(8,128)S(1)} %bitcast.112, bf16[8,512]{0,1:T(8,128)(2,1)S(1)} %copy-done.16, bf16[1,8,512,256]{3,2,1,0:T(8,128)(2,1)S(1)} %copy-done.9), kind=kLoop, calls=%fused_computation.28 | loop fusion | flops 4194304 | bytes 8396800 | tf_op jit(solution)/shard_map/convert_element_type | solution.py:157
  184.6 5.4 %all-to-all-done.1 = bf16[16,1,144,256]{3,2,1,0:T(8,128)(2,1)S(1)} async-done(((bf16[16,1,144,256]{3,2,1,0:T(8,128)(2,1)}), bf16[16,1,144,256]{3,2,1,0:T(8,128)(2,1)S(1)}, u32[]{:S(2)}, u32[]{:S(2)}) %all-to-all-start.1) | async-done | bytes 1179680 | tf_op jit(solution)/shard_map/all_to_all | solution.py:133
  190.4 11.0 %conditional.4 = (f32[2,1,2,144,256]{4,3,2,1,0:T(8,128)S(1)}) conditional(s32[]{:T(128)} %clamp.3, bf16[2,1,2,144,256]{4,3,2,1,0:T(8,128)(2,1)S(1)} %pad_maximum_fusion.3, bf16[2,1,2,144,256]{4,3,2,1,0:T(8,128)(2,1)S(1)} %pad_maximum_fusion.3, bf16[2,1,2,144,256]{4,3,2,1,0:T(8,128)(2,1)S(1)} %pad_maximum_fusion.3), branch_computations={%region_2.3_spmd, %region_3.4_spmd, %region_4.5_spmd} | conditional | flops 147456 | bytes 2064432
  192.0 9.3 %collective-permute-done = bf16[2,1,2,144,256]{4,3,2,1,0:T(8,128)(2,1)S(1)} collective-permute-done((bf16[2,1,2,144,256]{4,3,2,1,0:T(8,128)(2,1)S(1)}, bf16[2,1,2,144,256]{4,3,2,1,0:T(8,128)(2,1)S(1)}, u32[]{:S(2)}, u32[]{:S(2)}) %collective-permute-start) | collective-permute-done | bytes 294944 | tf_op jit(solution)/shard_map/cond/branch_0_fun/ppermute | solution.py:33
  (120 shorter events, 49.0 us)
Async XLA Ops:
  1.5 6.0 %copy-start.15 = (bf16[8,512]{0,1:T(8,128)(2,1)}, bf16[8,512]{0,1:T(8,128)(2,1)S(1)}, u32[]{:S(2)}) copy-start(bf16[8,512]{0,1:T(8,128)(2,1)S(1)} %copy.49) | copy-start | bytes 24580
  1.5 2.9 %copy-start.8 = (bf16[1,8,512,256]{3,2,1,0:T(8,128)(2,1)S(1)}, bf16[1,8,512,256]{3,2,1,0:T(8,128)(2,1)}, u32[]{:S(2)}) copy-start(bf16[1,8,512,256]{3,2,1,0:T(8,128)(2,1)} %param.10) | copy-start | bytes 6291460
  9.1 3.6 %copy-start.17 = (f32[1,2,144,256]{3,2,1,0:T(8,128)S(1)}, f32[1,2,144,256]{3,2,1,0:T(8,128)}, u32[]{:S(2)}) copy-start(f32[1,2,144,256]{3,2,1,0:T(8,128)} %param.12) | copy-start | bytes 884740
  9.2 18.1 %collective-permute-start.3 = (bf16[2,1,512,256]{3,2,1,0:T(8,128)(2,1)S(1)}, bf16[2,1,512,256]{3,2,1,0:T(8,128)(2,1)S(1)}, u32[]{:S(2)}, u32[]{:S(2)}) collective-permute-start(bf16[2,1,512,256]{3,2,1,0:T(8,128)(2,1)S(1)} %copy.52), channel_id=1, source_target_pairs={{0,1},{1,2},{2,3},{3,4},{4,5},{5,6},{6,7},{7,8},{8,9},{9,10},{10,1... | collective-permute-start | bytes 1572872 | tf_op jit(solution)/shard_map/ppermute | solution.py:17
  11.4 16.7 %collective-permute-start.4 = (bf16[2,1,512,256]{3,2,1,0:T(8,128)(2,1)}, bf16[2,1,512,256]{3,2,1,0:T(8,128)(2,1)}, u32[]{:S(2)}, u32[]{:S(2)}) collective-permute-start(bf16[2,1,512,256]{3,2,1,0:T(8,128)(2,1)} %copy.53), channel_id=1, source_target_pairs={{1,0},{2,1},{3,2},{4,3},{5,4},{6,5},{7,6},{8,7},{9,8},{10,9},{11,1... | collective-permute-start | bytes 1572872 | tf_op jit(solution)/shard_map/ppermute | solution.py:18
  14.4 76.5 %all-to-all-start = ((bf16[16,2,144,256]{3,2,1,0:T(8,128)(2,1)}), bf16[16,2,144,256]{3,2,1,0:T(8,128)(2,1)}, u32[]{:S(2)}, u32[]{:S(2)}) async-start(bf16[16,2,144,256]{3,2,1,0:T(8,128)(2,1)} %broadcast_in_dim.9), calls=%async_computation | async-start | bytes 4718592 | tf_op jit(solution)/shard_map/all_to_all | solution.py:125
  27.3 2.7 %copy-start.5 = (bf16[1,8,512,256]{3,1,2,0:T(8,128)(2,1)S(1)}, bf16[1,8,512,256]{3,1,2,0:T(8,128)(2,1)}, u32[]{:S(2)}) copy-start(bf16[1,8,512,256]{3,1,2,0:T(8,128)(2,1)} %copy-done.4) | copy-start | bytes 6291460
  38.5 2.1 %copy-start = (bf16[10,1,512,256]{3,0,2,1:T(8,128)(2,1)}, bf16[10,1,512,256]{3,0,2,1:T(8,128)(2,1)S(1)}, u32[]{:S(2)}) copy-start(bf16[10,1,512,256]{3,0,2,1:T(8,128)(2,1)S(1)} %get-tuple-element.26) | copy-start | bytes 7864324
  46.7 4.9 %copy-start.2 = (bf16[10,1,512,256]{3,0,2,1:T(8,128)(2,1)S(1)}, bf16[10,1,512,256]{3,0,2,1:T(8,128)(2,1)}, u32[]{:S(2)}) copy-start(bf16[10,1,512,256]{3,0,2,1:T(8,128)(2,1)} %get-tuple-element.27) | copy-start | bytes 7864324
  51.6 2.2 %copy-start.1 = (bf16[10,1,512,256]{3,0,2,1:T(8,128)(2,1)S(1)}, bf16[10,1,512,256]{3,0,2,1:T(8,128)(2,1)}, u32[]{:S(2)}) copy-start(bf16[10,1,512,256]{3,0,2,1:T(8,128)(2,1)} %copy-done) | copy-start | bytes 7864324
  63.0 8.8 %slice-start.2 = ((s8[4259840]{0:T(1024)(128)(4,1)}), s8[65536]{0:T(1024)(128)(4,1)S(1)}, s32[]{:S(2)}) async-start(s8[4259840]{0:T(1024)(128)(4,1)} %bitcast.108), calls=%async_computation.5 | async-start | bytes 131072
  67.3 4.5 %slice-start.3 = ((s8[4259840]{0:T(1024)(128)(4,1)}), s8[4194304]{0:T(1024)(128)(4,1)S(1)}, s32[]{:S(2)}) async-start(s8[4259840]{0:T(1024)(128)(4,1)} %bitcast.108), calls=%async_computation.6 | async-start | bytes 8388608
  71.8 1.8 copy-start.7
  73.6 2.6 %copy-start.3 = (bf16[10,1,8,65,256]{4,3,2,0,1:T(8,128)(2,1)S(1)}, bf16[10,1,8,65,256]{4,3,2,0,1:T(8,128)(2,1)}, u32[]{:S(2)}) copy-start(bf16[10,1,8,65,256]{4,3,2,0,1:T(8,128)(2,1)} %reshape.83) | copy-start | bytes 7987204
  76.2 5.6 %slice-start = ((s8[4259840]{0:T(1024)(128)(4,1)}), s8[4194304]{0:T(1024)(128)(4,1)S(1)}, s32[]{:S(2)}) async-start(s8[4259840]{0:T(1024)(128)(4,1)} %bitcast.105), calls=%async_computation.3 | async-start | bytes 8388608
  78.2 3.7 %slice-start.1 = ((s8[4259840]{0:T(1024)(128)(4,1)}), s8[65536]{0:T(1024)(128)(4,1)S(1)}, s32[]{:S(2)}) async-start(s8[4259840]{0:T(1024)(128)(4,1)} %bitcast.105), calls=%async_computation.4 | async-start | bytes 131072
  82.9 2.9 %copy-start.10 = (bf16[10,1,8,65,256]{4,2,3,0,1:T(8,128)(2,1)}, bf16[10,1,8,65,256]{4,2,3,0,1:T(8,128)(2,1)S(1)}, u32[]{:S(2)}) copy-start(bf16[10,1,8,65,256]{4,2,3,0,1:T(8,128)(2,1)S(1)} %copy.58) | copy-start | bytes 7987204
  93.7 5.4 %copy-start.19 = (bf16[1,16,144,256]{3,2,0,1:T(8,128)(2,1)}, bf16[1,16,144,256]{3,2,0,1:T(8,128)(2,1)S(1)}, u32[]{:S(2)}) copy-start(bf16[1,16,144,256]{3,2,0,1:T(8,128)(2,1)S(1)} %get-tuple-element.39) | copy-start | bytes 3538948
  93.7 5.4 %copy-start.12 = (bf16[10,8,65,256,1]{3,1,4,2,0:T(8,128)(2,1)S(1)}, bf16[10,8,65,256,1]{3,1,4,2,0:T(8,128)(2,1)}, u32[]{:S(2)}) copy-start(bf16[10,8,65,256,1]{3,1,4,2,0:T(8,128)(2,1)} %copy.85) | copy-start | bytes 7987204
  93.7 5.4 %copy-start.13 = (bf16[10,8,65,256,1]{3,1,4,2,0:T(8,128)(2,1)S(1)}, bf16[10,8,65,256,1]{3,1,4,2,0:T(8,128)(2,1)}, u32[]{:S(2)}) copy-start(bf16[10,8,65,256,1]{3,1,4,2,0:T(8,128)(2,1)} %get-tuple-element.48) | copy-start | bytes 7987204
  93.7 5.5 %copy-start.14 = (bf16[10,8,65,256,1]{3,1,4,2,0:T(8,128)(2,1)S(1)}, bf16[10,8,65,256,1]{3,1,4,2,0:T(8,128)(2,1)}, u32[]{:S(2)}) copy-start(bf16[10,8,65,256,1]{3,1,4,2,0:T(8,128)(2,1)} %get-tuple-element.49) | copy-start | bytes 7987204
  93.7 5.5 %copy-start.23 = (pred[8,65]{0,1:T(8,128)(4,1)S(1)}, pred[8,65]{0,1:T(8,128)(4,1)}, u32[]{:S(2)}) copy-start(pred[8,65]{0,1:T(8,128)(4,1)} %constant.57) | copy-start | bytes 1564
  99.1 8.7 %copy-start.24 = (f32[8,8,65,256]{3,1,2,0:T(8,128)}, f32[8,8,65,256]{3,1,2,0:T(8,128)S(1)}, u32[]{:S(2)}) copy-start(f32[8,8,65,256]{3,1,2,0:T(8,128)S(1)} %fusion.27) | copy-start | bytes 12779524
  108.0 8.9 %copy-start.22 = (bf16[10,1,7,2,256]{4,2,3,0,1:T(8,128)(2,1)S(1)}, bf16[10,1,7,2,256]{4,2,3,0,1:T(8,128)(2,1)}, u32[]{:S(2)}) copy-start(bf16[10,1,7,2,256]{4,2,3,0,1:T(8,128)(2,1)} %slice.60) | copy-start | bytes 215044
  109.5 51.9 %all-to-all-start.2 = ((bf16[16,1,144,256]{3,2,1,0:T(8,128)(2,1)}), bf16[16,1,144,256]{3,2,1,0:T(8,128)(2,1)S(1)}, u32[]{:S(2)}, u32[]{:S(2)}) async-start(bf16[16,1,144,256]{3,2,1,0:T(8,128)(2,1)} %bitcast.31), calls=%async_computation.2 | async-start | bytes 2359296 | tf_op jit(solution)/shard_map/all_to_all | solution.py:133
  132.1 21.6 %collective-permute-start.6 = (bf16[1,1,512,256]{3,1,2,0:T(2,128)(2,1)}, bf16[1,1,512,256]{3,1,2,0:T(2,128)(2,1)}, u32[]{:S(2)}, u32[]{:S(2)}) collective-permute-start(bf16[1,1,512,256]{3,1,2,0:T(2,128)(2,1)} %slice.69), channel_id=1, source_target_pairs={{1,0},{2,1},{3,2},{4,3},{5,4},{6,5},{7,6},{8,7},{9,8},{10,9},{11,1... | collective-permute-start | bytes 786440 | tf_op jit(solution)/shard_map/ppermute | solution.py:18
  137.9 15.5 %collective-permute-start.5 = (bf16[1,1,512,256]{3,2,1,0:T(8,128)(2,1)S(1)}, bf16[1,1,512,256]{3,2,1,0:T(8,128)(2,1)S(1)}, u32[]{:S(2)}, u32[]{:S(2)}) collective-permute-start(bf16[1,1,512,256]{3,2,1,0:T(8,128)(2,1)S(1)} %slice.66), channel_id=1, source_target_pairs={{0,1},{1,2},{2,3},{3,4},{4,5},{5,6},{6,7},{7,8},{8,9},{9,10},{10,1... | collective-permute-start | bytes 786440 | tf_op jit(solution)/shard_map/ppermute | solution.py:17
  158.2 12.4 %copy-start.20 = (bf16[1,16,144,256]{3,2,0,1:T(8,128)(2,1)S(1)}, bf16[1,16,144,256]{3,2,0,1:T(8,128)(2,1)}, u32[]{:S(2)}) copy-start(bf16[1,16,144,256]{3,2,0,1:T(8,128)(2,1)} %copy-done.19) | copy-start | bytes 3538948
  161.4 28.7 %all-to-all-start.1 = ((bf16[16,1,144,256]{3,2,1,0:T(8,128)(2,1)}), bf16[16,1,144,256]{3,2,1,0:T(8,128)(2,1)S(1)}, u32[]{:S(2)}, u32[]{:S(2)}) async-start(bf16[16,1,144,256]{3,2,1,0:T(8,128)(2,1)} %bitcast.23), calls=%async_computation.1 | async-start | bytes 2359296 | tf_op jit(solution)/shard_map/all_to_all | solution.py:133
  182.7 7.5 %copy-start.18 = (f32[1,2,144,256]{3,2,1,0:T(8,128)S(1)}, f32[1,2,144,256]{3,2,1,0:T(8,128)}, u32[]{:S(2)}) copy-start(f32[1,2,144,256]{3,2,1,0:T(8,128)} %param.12) | copy-start | bytes 884740
  182.7 7.5 %copy-start.21 = (f32[1,2,144,256]{3,2,1,0:T(8,128)S(1)}, f32[1,2,144,256]{3,2,1,0:T(8,128)}, u32[]{:S(2)}) copy-start(f32[1,2,144,256]{3,2,1,0:T(8,128)} %param.13) | copy-start | bytes 884740
  190.4 10.9 %collective-permute-start = (bf16[2,1,2,144,256]{4,3,2,1,0:T(8,128)(2,1)S(1)}, bf16[2,1,2,144,256]{4,3,2,1,0:T(8,128)(2,1)S(1)}, u32[]{:S(2)}, u32[]{:S(2)}) collective-permute-start(bf16[2,1,2,144,256]{4,3,2,1,0:T(8,128)(2,1)S(1)} %param), channel_id=1, source_target_pairs={{0,16},{16,32},{32,48},{48,64},{64,80},{80,96},{96,112},{112,0},{1... | collective-permute-start | bytes 884744 | tf_op jit(solution)/shard_map/cond/branch_0_fun/ppermute | solution.py:33
  (5 other events, 8.1 us)
where the time goes:
time: 206 us; the launch traced here: 202 us
  local copies, waits for them, and re-layouts  81 us (39%)
  matrix products  42.7 us (21%)
  starting transfers between devices  37.4 us (18%)
  other arithmetic  24.4 us (12%)
  waiting for transfers between devices  14.7 us (7%)
  between operations  2.2 us (1%)
    unnamed x70, local copies, waits for them, and re-layouts  18.8 us
    slice x8, local copies, waits for them, and re-layouts, shards(): masked_ext = paired[1]  18.4 us
    conv_general_dilated x2, matrix products, conv_behind(): lax.conv_general_dilated(extended[None], taps, (1, 1), ((0, 0), (1, 1)),...  16.9 us
    all_to_all x2, starting transfers between devices, scattered(): lax.all_to_all(jnp.moveaxis(blocks, 1, 0).astype(jnp.bfloat16), 'space',...  16.6 us
    slice x7, local copies, waits for them, and re-layouts, shards(): input_ext = paired[0]  15.8 us
    all_to_all x1, starting transfers between devices, gathered_kernels(): have = lax.all_to_all(copies, 'space', 0, 0, tiled=True)  12.3 us
    conv_general_dilated x1, matrix products, kernel_grad(): lax.conv_general_dilated(extended[None], upstream[None], (1, 1), ((0, 0),...  11.8 us
    convert_element_type x9, local copies, waits for them, and re-layouts, shards(): (conv_behind(masked_ext, kernel_second) * silu_slope(preact)).astype(jnp....  10.7 us
  transfers between devices with their start and end apart: 8, of which 2 were waited for; matrix products, arithmetic and copies ran while one was open for 56% of the time, Pallas kernels for 0%

commit v1 on v0

--- a/solution.py
+++ b/solution.py
@@ -84,6 +84,38 @@
     return grad.reshape(-1, grad.shape[-1])
 
 
+def both_ahead(extended, kernel_first, kernel_second):
+    chan_count = kernel_first.shape[1]
+    first = kernel_first.reshape(3, 3, -1, chan_count)
+    second = jnp.flip(kernel_second.reshape(3, 3, -1, chan_count), (0, 1)).transpose(0, 1, 3, 2)
+    summed = lax.conv_general_dilated(
+        extended[None],
+        jnp.concatenate([first, second], axis=-1),
+        (1, 1),
+        ((0, 0), (1, 1)),
+        dimension_numbers=("NHWC", "HWIO", "NHWC"),
+        feature_group_count=2,
+        preferred_element_type=jnp.float32,
+    )[0]
+    return summed[..., :chan_count], summed[..., chan_count:]
+
+
+def both_grads(extended, upstream):
+    chan_count = extended.shape[-1] // 2
+    grad = lax.conv_general_dilated(
+        extended[None],
+        upstream[None],
+        (1, 1),
+        ((0, 0), (1, 1)),
+        dimension_numbers=("CHWN", "IHWO", "HWNC"),
+        batch_group_count=2,
+        preferred_element_type=jnp.float32,
+    )
+    first = grad[..., :chan_count]
+    second = jnp.flip(grad[..., chan_count:], (0, 1)).transpose(0, 1, 3, 2)
+    return jnp.stack([first.reshape(-1, chan_count), second.reshape(-1, chan_count)])
+
+
 def silu_slope(preact):
     sigma = jax.nn.sigmoid(preact)
     return sigma * (1.0 + preact * (1.0 - sigma))
@@ -145,19 +177,16 @@
     kernels = gathered_kernels(weights)
     kernel_first = kernels[0]
     kernel_second = kernels[1]
-    paired = rim(jnp.stack([inputs[0], masked]))
-    input_ext = paired[0]
-    masked_ext = paired[1]
-    preact = conv_ahead(input_ext, kernel_first)
+    paired = rim(jnp.concatenate([inputs[0], masked], axis=-1)[None])[0]
+    preact, back_hidden = both_ahead(paired, kernel_first, kernel_second)
     hidden = jax.nn.silu(preact).astype(jnp.bfloat16)
-    share_second = scattered(kernel_grad_behind(masked_ext, hidden)[None] * scale)
-    back_mid = (conv_behind(masked_ext, kernel_second) * silu_slope(preact)).astype(jnp.bfloat16)
-    grad_first = kernel_grad(input_ext, back_mid) * scale
-    back_ext, grad_first = lax.optimization_barrier((rim(back_mid[None])[0], grad_first))
+    back_mid = (back_hidden * silu_slope(preact)).astype(jnp.bfloat16)
+    grads = both_grads(paired, jnp.concatenate([back_mid, hidden], axis=-1)) * scale
+    back_ext, grads = lax.optimization_barrier((rim(back_mid[None])[0], grads))
     grad_input = (conv_behind(back_ext, kernel_first) + masked.astype(jnp.float32)).astype(
         jnp.bfloat16
     )[None]
-    shares = jnp.stack([scattered(grad_first[None])[0], share_second[0]])[None]
+    shares = scattered(grads)[None]
     moment = 0.9 * momentum + shares
     updated = weights - 0.01 * moment
     mixed = gossip(step, jnp.stack([updated, moment]), send_both)

time: 206 us -> 396 us (1.92)
  the two profiles are of different devices: /device:TPU:0 before, /device:TPU:2 now
where the time goes in v1:
time: 396 us; the launch traced here: 389 us
  matrix products  177 us (45%)
  local copies, waits for them, and re-layouts  125 us (32%)
  other arithmetic  40.7 us (10%)
  starting transfers between devices  34.8 us (9%)
  waiting for transfers between devices  9.35 us (2%)
    conv_general_dilated x1, matrix products, both_grads(): lax.conv_general_dilated(extended[None], upstream[None], (1, 1), ((0, 0),...  86.4 us
    conv_general_dilated x1, matrix products, both_ahead(): lax.conv_general_dilated(extended[None], jnp.concatenate([first, second],...  83.2 us
    concatenate x3, local copies, waits for them, and re-layouts, extended_2(): shard = jnp.concatenate([before, shard, after], axis=dim)  26.3 us
    unnamed x26, local copies, waits for them, and re-layouts  24.8 us
    squeeze x1, local copies, waits for them, and re-layouts, both_ahead(): lax.conv_general_dilated(extended[None], jnp.concatenate([first, second],...  20.6 us
    concatenate x1, other arithmetic, extended_2(): shard = jnp.concatenate([before, shard, after], axis=dim)  20.5 us
    broadcast_in_dim x1, local copies, waits for them, and re-layouts, both_grads(): upstream[None]  20.3 us
    conv_general_dilated x4, local copies, waits for them, and re-layouts, conv_behind(): lax.conv_general_dilated(extended[None], taps, (1, 1), ((0, 0), (1, 1)),...  17.6 us
  transfers between devices with their start and end apart: 7, of which 2 were waited for; matrix products, arithmetic and copies ran while one was open for 22% of the time, Pallas kernels for 0%

profile of v1, /device:TPU:2, one launch (start us, length us, event | category | flops | bytes accessed | tf_op | source)
XLA Modules:
  0.0 388.8 jit_solution(11940635496392189401)
XLA Ops:
  1.4 2.9 copy.27
  4.2 3.9 %copy.26 = bf16[1,8,512,256]{2,3,1,0:T(8,128)(2,1)} copy(bf16[1,8,512,256]{3,2,1,0:T(8,128)(2,1)} %param.9) | data formatting | bytes 4194304 | tf_op args[0]
  9.8 2.3 pad_maximum_fusion.1
  12.9 1.9 collective-permute-start.3
  14.8 3.6 collective-permute-start.4
  20.2 9.3 %all-to-all-start = ((bf16[16,2,144,256]{3,2,1,0:T(8,128)(2,1)}), bf16[16,2,144,256]{3,2,1,0:T(8,128)(2,1)S(1)}, u32[]{:S(2)}, u32[]{:S(2)}) async-start(bf16[16,2,144,256]{3,2,1,0:T(8,128)(2,1)} %broadcast_in_dim.27), calls=%async_computation | async-start | bytes 4718592 | tf_op jit(solution)/shard_map/all_to_all | solution.py:157
  29.5 20.3 %copy.29 = bf16[1,8,512,2,256]{4,0,3,2,1:T(2,128)(2,1)} copy(bf16[1,8,512,2,256]{2,4,3,1,0:T(8,128)(2,1)} %bitcast.76) | data formatting | bytes 8388608 | tf_op jit(solution)/shard_map/concatenate | solution.py:19
  50.6 2.4 copy.28
  53.0 3.6 copy.30
  56.6 20.5 %pad_maximum_fusion = bf16[1,10,512,2,256]{4,0,3,2,1:T(2,128)(2,1)} fusion(bf16[1,1,512,2,256]{4,0,3,2,1:T(2,128)(2,1)} %copy.30, bf16[1,8,512,2,256]{4,0,3,2,1:T(2,128)(2,1)} %copy.29, bf16[1,1,512,2,256]{4,0,3,2,1:T(2,128)(2,1)S(1)} %copy.28), kind=kLoop, calls=%fused_computation | loop fusion | flops 5242880 | bytes 10485760 | tf_op jit(solution)/shard_map/concatenate | solution.py:19
  78.6 83.2 %fusion.11 = f32[1,8,512,2,256]{4,0,3,2,1:T(1,128)} fusion(bf16[1,10,512,2,256]{4,0,3,2,1:T(2,128)(2,1)} %pad_maximum_fusion, bf16[3,3,256,2,256]{4,2,3,1,0:T(8,128)(2,1)S(1)} %pad_maximum_fusion.8), kind=kOutput, calls=%fused_computation.24 | convolution fusion | flops 9651093504 | bytes 15990784 | tf_op jit(solution)/shard_map/conv_general_dilated | solution.py:91
  161.8 20.6 %copy.45 = f32[1,8,512,2,256]{2,4,3,1,0:T(8,128)} copy(f32[1,8,512,2,256]{4,0,3,2,1:T(1,128)} %fusion.11) | data formatting | bytes 16777216 | tf_op jit(solution)/shard_map/squeeze | solution.py:91
  182.4 4.3 %multiply_convert_fusion = (bf16[8,512,256]{1,2,0:T(8,128)(2,1)S(1)}, bf16[8,512,256]{1,2,0:T(8,128)(2,1)S(1)}) fusion(f32[8,512,512]{1,2,0:T(8,128)} %bitcast.72), kind=kLoop, calls=%fused_computation.12 | loop fusion | flops 11534336 | bytes 12582912 | tf_op jit(solution)/shard_map/convert_element_type | solution.py:182
  186.7 2.4 pad_maximum_fusion.2
  189.2 20.3 %copy.35 = bf16[1,8,512,2,256]{4,0,3,2,1:T(2,128)(2,1)} copy(bf16[1,8,512,2,256]{2,4,3,1,0:T(8,128)(2,1)} %bitcast.77) | data formatting | bytes 8388608 | tf_op jit(solution)/shard_map/broadcast_in_dim | solution.py:107
  209.5 86.4 %fusion.25 = f32[3,3,256,2,256]{2,4,3,1,0:T(8,128)S(1)} fusion(bf16[1,10,512,2,256]{4,0,3,2,1:T(2,128)(2,1)} %pad_maximum_fusion, bf16[1,8,512,2,256]{4,0,3,2,1:T(2,128)(2,1)} %copy.35), kind=kOutput, calls=%fused_computation.47 | convolution fusion | flops 9651093504 | bytes 14155776 | tf_op jit(solution)/shard_map/conv_general_dilated | solution.py:105
  295.9 2.6 fusion.21
  298.5 13.8 %copy.48 = f32[3,3,256,256]{3,2,1,0:T(8,128)} copy(f32[3,3,256,256]{2,3,1,0:T(8,128)} %get-tuple-element.28) | data formatting | bytes 4718592
  312.3 3.3 rev.10
  315.6 2.0 collective-permute-start.5
  317.7 3.5 collective-permute-start.6
  321.2 2.8 maximum_multiply_fusion
  328.6 11.1 %all-to-all-start.1 = ((bf16[16,2,144,256]{3,2,1,0:T(8,128)(2,1)}), bf16[16,2,144,256]{3,2,1,0:T(8,128)(2,1)}, u32[]{:S(2)}, u32[]{:S(2)}) async-start(bf16[16,2,144,256]{3,2,1,0:T(8,128)(2,1)} %bitcast.70), calls=%async_computation.1 | async-start | bytes 4718592 | tf_op jit(solution)/shard_map/all_to_all | solution.py:165
  340.6 3.4 pad
  343.9 6.7 %reshape.44 = bf16[10,1,8,65,256]{3,2,4,0,1:T(8,128)(2,1)} reshape(bf16[10,1,520,256]{2,3,0,1:T(8,128)(2,1)S(1)} %pad) | data formatting | bytes 5324800 | tf_op jit(solution)/shard_map/conv_general_dilated | solution.py:52
  350.7 8.6 %copy.39 = bf16[10,1,8,65,256]{4,2,3,0,1:T(8,128)(2,1)} copy(bf16[10,1,8,65,256]{3,2,4,0,1:T(8,128)(2,1)} %reshape.44) | data formatting | bytes 5324800 | tf_op jit(solution)/shard_map/conv_general_dilated | solution.py:52
  360.2 7.2 %broadcast_select_fusion = f32[8,8,65,256]{3,1,2,0:T(8,128)S(1)} fusion(pred[8,65]{0,1:T(8,128)(4,1)S(1)} %copy-done.10, bf16[3,3,256,256]{3,2,1,0:T(8,128)(2,1)S(1)} %bitcast.87, bf16[10,1,7,2,256]{4,2,3,0,1:T(8,128)(2,1)S(1)} %slice.62, bf16[10,1,8,65,256]{4,2,3,0,1:T(8,128)(2,1)} %copy.39), kind=kOutput, calls=%fused_computation.25 | convolution fusion | flops 4916633600 | bytes 8174088 | tf_op jit(solution)/shard_map/conv_general_dilated | solution.py:52
  369.0 3.1 fusion.2
  373.9 2.0 convert_reduce_fusion
  376.1 11.6 %conditional.4 = (f32[2,1,2,144,256]{4,3,2,1,0:T(8,128)S(1)}) conditional(s32[]{:T(128)} %clamp.3, bf16[2,1,2,144,256]{4,3,2,1,0:T(8,128)(2,1)S(1)} %pad_maximum_fusion.5, bf16[2,1,2,144,256]{4,3,2,1,0:T(8,128)(2,1)S(1)} %pad_maximum_fusion.5, bf16[2,1,2,144,256]{4,3,2,1,0:T(8,128)(2,1)S(1)} %pad_maximum_fusion.5), branch_computations={%region_1.2_spmd, %region_2.3_spmd, %region_3.4_spmd} | conditional | flops 147456 | bytes 2064432
  376.1 3.3 collective-permute-start.1
  379.4 8.3 %collective-permute-done.1 = bf16[2,1,2,144,256]{4,3,2,1,0:T(8,128)(2,1)S(1)} collective-permute-done((bf16[2,1,2,144,256]{4,3,2,1,0:T(8,128)(2,1)S(1)}, bf16[2,1,2,144,256]{4,3,2,1,0:T(8,128)(2,1)S(1)}, u32[]{:S(2)}, u32[]{:S(2)}) %collective-permute-start.1) | collective-permute-done | bytes 294944 | tf_op jit(solution)/shard_map/cond/branch_1_fun/ppermute | solution.py:33
  (50 shorter events, 17.1 us)
Async XLA Ops:
  1.4 6.8 %copy-start.8 = (bf16[8,512]{1,0:T(8,128)(2,1)}, bf16[8,512]{1,0:T(8,128)(2,1)S(1)}, u32[]{:S(2)}) copy-start(bf16[8,512]{1,0:T(8,128)(2,1)S(1)} %convert_element_type.59) | copy-start | bytes 24580
  8.2 1.6 copy-start.1
  9.7 8.7 %copy-start.4 = (f32[1,2,144,256]{3,2,1,0:T(8,128)S(1)}, f32[1,2,144,256]{3,2,1,0:T(8,128)}, u32[]{:S(2)}) copy-start(f32[1,2,144,256]{3,2,1,0:T(8,128)} %param.12) | copy-start | bytes 884740
  12.9 36.9 %collective-permute-start.3 = (bf16[1,1,512,512]{2,3,1,0:T(8,128)(2,1)S(1)}, bf16[1,1,512,512]{2,3,1,0:T(8,128)(2,1)S(1)}, u32[]{:S(2)}, u32[]{:S(2)}) collective-permute-start(bf16[1,1,512,512]{2,3,1,0:T(8,128)(2,1)S(1)} %get-tuple-element.30), channel_id=1, source_target_pairs={{0,1},{1,2},{2,3},{3,4},{4,5},{5,6},{6,7},{7,8},{8,9},{9,10},{10,1... | collective-permute-start | bytes 1572872 | tf_op jit(solution)/shard_map/ppermute | solution.py:17
  14.8 38.2 %collective-permute-start.4 = (bf16[1,1,512,512]{2,3,1,0:T(8,128)(2,1)}, bf16[1,1,512,512]{2,3,1,0:T(8,128)(2,1)}, u32[]{:S(2)}, u32[]{:S(2)}) collective-permute-start(bf16[1,1,512,512]{2,3,1,0:T(8,128)(2,1)} %get-tuple-element.31), channel_id=1, source_target_pairs={{1,0},{2,1},{3,2},{4,3},{5,4},{6,5},{7,6},{8,7},{9,8},{10,9},{11,1... | collective-permute-start | bytes 1572872 | tf_op jit(solution)/shard_map/ppermute | solution.py:18
  20.2 57.0 %all-to-all-start = ((bf16[16,2,144,256]{3,2,1,0:T(8,128)(2,1)}), bf16[16,2,144,256]{3,2,1,0:T(8,128)(2,1)S(1)}, u32[]{:S(2)}, u32[]{:S(2)}) async-start(bf16[16,2,144,256]{3,2,1,0:T(8,128)(2,1)} %broadcast_in_dim.27), calls=%async_computation | async-start | bytes 4718592 | tf_op jit(solution)/shard_map/all_to_all | solution.py:157
  49.8 0.8 copy-start.6
  77.5 1.1 copy-start.2
  315.6 8.4 %collective-permute-start.5 = (bf16[1,1,512,256]{2,3,1,0:T(8,128)(2,1)S(1)}, bf16[1,1,512,256]{2,3,1,0:T(8,128)(2,1)S(1)}, u32[]{:S(2)}, u32[]{:S(2)}) collective-permute-start(bf16[1,1,512,256]{2,3,1,0:T(8,128)(2,1)S(1)} %get-tuple-element.36), channel_id=1, source_target_pairs={{0,1},{1,2},{2,3},{3,4},{4,5},{5,6},{6,7},{7,8},{8,9},{9,10},{10,1... | collective-permute-start | bytes 786440 | tf_op jit(solution)/shard_map/ppermute | solution.py:17
  317.7 7.4 %collective-permute-start.6 = (bf16[1,1,512,256]{2,3,1,0:T(8,128)(2,1)S(1)}, bf16[1,1,512,256]{2,3,1,0:T(8,128)(2,1)S(1)}, u32[]{:S(2)}, u32[]{:S(2)}) collective-permute-start(bf16[1,1,512,256]{2,3,1,0:T(8,128)(2,1)S(1)} %get-tuple-element.37), channel_id=1, source_target_pairs={{1,0},{2,1},{3,2},{4,3},{5,4},{6,5},{7,6},{8,7},{9,8},{10,9},{11,1... | collective-permute-start | bytes 786440 | tf_op jit(solution)/shard_map/ppermute | solution.py:18
  328.6 11.8 %copy-start.9 = (bf16[8,512]{1,0:T(8,128)(2,1)S(1)}, bf16[8,512]{1,0:T(8,128)(2,1)}, u32[]{:S(2)}) copy-start(bf16[8,512]{1,0:T(8,128)(2,1)} %copy-done.8) | copy-start | bytes 24580
  328.6 45.3 %all-to-all-start.1 = ((bf16[16,2,144,256]{3,2,1,0:T(8,128)(2,1)}), bf16[16,2,144,256]{3,2,1,0:T(8,128)(2,1)}, u32[]{:S(2)}, u32[]{:S(2)}) async-start(bf16[16,2,144,256]{3,2,1,0:T(8,128)(2,1)} %bitcast.70), calls=%async_computation.1 | async-start | bytes 4718592 | tf_op jit(solution)/shard_map/all_to_all | solution.py:165
  350.7 9.5 %copy-start.3 = (bf16[1,16,144,256]{3,2,1,0:T(8,128)(2,1)S(1)}, bf16[1,16,144,256]{3,2,1,0:T(8,128)(2,1)}, u32[]{:S(2)}) copy-start(bf16[1,16,144,256]{3,2,1,0:T(8,128)(2,1)} %copy-done.2) | copy-start | bytes 3538948
  350.7 9.5 %copy-start.10 = (pred[8,65]{0,1:T(8,128)(4,1)S(1)}, pred[8,65]{0,1:T(8,128)(4,1)}, u32[]{:S(2)}) copy-start(pred[8,65]{0,1:T(8,128)(4,1)} %constant.40) | copy-start | bytes 1564
  367.4 1.6 copy-start
  372.1 3.8 copy-start.5
  372.1 3.8 copy-start.7
  376.1 11.5 %collective-permute-start.1 = (bf16[2,1,2,144,256]{4,3,2,1,0:T(8,128)(2,1)S(1)}, bf16[2,1,2,144,256]{4,3,2,1,0:T(8,128)(2,1)S(1)}, u32[]{:S(2)}, u32[]{:S(2)}) collective-permute-start(bf16[2,1,2,144,256]{4,3,2,1,0:T(8,128)(2,1)S(1)} %param.1), channel_id=1, source_target_pairs={{0,32},{16,48},{32,64},{48,80},{64,96},{80,112},{96,0},{112,16},{1... | collective-permute-start | bytes 884744 | tf_op jit(solution)/shard_map/cond/branch_1_fun/ppermute | solution.py:33
